TPU v7x, 32 devices: a whole 2x2x4 slice. The times are simulated.
32 devices in a mesh: groups: 2 (over y), prompt: 4 (over x, core), resp: 4 (over z).
Axes of the slice: x: 2, y: 2, z: 4, core: 2. Of those that a mesh axis runs over, the one named last changes fastest.
Arguments:
- queries: bfloat16 [8, 4, 32, 8192], P(('groups', 'prompt'), 'resp'), parts along dimension 0, may hold values from -90 to 90
- cotangent: bfloat16 [8, 4, 32, 8192], P(('groups', 'prompt'), 'resp'), parts along dimension 0, may hold values from -6 to 6
- resp_keys: bfloat16 [8, 4, 32, 512], P(('groups', 'prompt'), 'resp'), parts along dimension 0, may hold values from -6 to 6
- resp_values: bfloat16 [8, 4, 32, 512], P(('groups', 'prompt'), 'resp'), parts along dimension 0, may hold values from -6 to 6
- prefix_keys: bfloat16 [8, 512, 512], P(('groups', 'prompt'), 'resp'), parts along dimension 0, may hold values from -5 to 5
- prefix_values: bfloat16 [8, 512, 512], P(('groups', 'prompt'), 'resp'), parts along dimension 0, may hold values from -6 to 6
- counts: int32 [8], P(('groups', 'prompt')), parts along dimension 0, may hold values from 1 to 4, as said below
- lengths: int32 [8, 4], P(('groups', 'prompt'), 'resp'), parts along dimension 0, may hold values from 8 to 32, as said below
- policy_likelihood: float32 [8, 4], P(('groups', 'prompt'), 'resp'), parts along dimension 0, may hold values from -8 to 8
- reference_likelihood: float32 [8, 4], P(('groups', 'prompt'), 'resp'), parts along dimension 0, may hold values from -8 to 8
Outputs:
- grad_queries: bfloat16 [8, 4, 32, 8192], P(('groups', 'prompt'), 'resp'), parts along dimension 0
- grad_resp_keys: bfloat16 [8, 4, 32, 512], P(('groups', 'prompt'), 'resp'), parts along dimension 0
- grad_resp_values: bfloat16 [8, 4, 32, 512], P(('groups', 'prompt'), 'resp'), parts along dimension 0
- grad_prefix_keys: bfloat16 [8, 512, 512], P(('groups', 'prompt'), 'resp'), parts along dimension 0
- grad_prefix_values: bfloat16 [8, 512, 512], P(('groups', 'prompt'), 'resp'), parts along dimension 0
- forget_loss: float32 [8], P(('groups', 'prompt')), parts along dimension 0
There are 2 independent parts, one for each index of `groups`. A program takes and returns all parts, laid end to end along the dimension named above; each array names one. Nothing has to cross between parts.
Inputs may be any that keep to these rules, and one draw needn't show every extreme that they name: `counts`: live responses of a prompt fill its first slots; some prompt has all 4. `lengths`: tokens of a response are its first slots, the rest padding; each prompt has a live response of 32 tokens.
All inputs are finite; a program needn't handle non-finite values.
Results may differ from a plain program's by a relative error of at most 0.0085.
Values may be sent and summed in bfloat16 or wider, within the bound.
No kernel may reach another device: no remote copies, remote signals or barrier semaphores. Data moves between devices by JAX's collectives and lax.ppermute only.
A program may use at most 128 MiB of HBM per device.

v0:
```python
import math
import jax
import jax.numpy as jnp
from jax import lax
from jax.sharding import PartitionSpec as P

HEADS = 64
KV_HEADS = 4
HEAD_DIM = 128
loss_beta = 0.5
masked_score = -1e30


def head_block(values_in, position, column_span):
    return lax.slice_in_dim(
        values_in, position * column_span, (position + 1) * column_span, axis=values_in.ndim - 1
    )


def across_rows(left_side, right_side):
    return lax.dot_general(
        left_side, right_side, (((1,), (1,)), ((), ())), preferred_element_type=jnp.float32
    )


def down_columns(left_side, right_side):
    return lax.dot_general(
        left_side, right_side, (((0,), (0,)), ((), ())), preferred_element_type=jnp.float32
    )


def own_scores(query_four, own_keys, scaling):
    resp_len = own_keys.shape[1]
    scores = (
        jnp.einsum("sqgd,skd->sqgk", query_four, own_keys, preferred_element_type=jnp.float32)
        * scaling
    )
    positions = jnp.arange(resp_len, dtype=jnp.int32)
    causal = positions[:, None] >= positions[None, :]
    return jnp.where(causal[None, :, None, :], scores, masked_score).reshape(-1, resp_len)


def own_slopes(grad_four, own_values):
    resp_len = own_values.shape[1]
    return jnp.einsum(
        "sqgd,skd->sqgk", grad_four, own_values, preferred_element_type=jnp.float32
    ).reshape(-1, resp_len)


def own_grads(shift_own, weights_own, query_four, grad_four, own_keys, scaling):
    four_shape = query_four.shape[:3] + (own_keys.shape[1],)
    shift_four = shift_own.reshape(four_shape)
    weight_four = weights_own.astype(jnp.bfloat16).reshape(four_shape)
    query_grad = (
        jnp.einsum("sqgk,skd->sqgd", shift_four, own_keys, preferred_element_type=jnp.float32)
        * scaling
    )
    key_grad = (
        jnp.einsum("sqgk,sqgd->skd", shift_four, query_four, preferred_element_type=jnp.float32)
        * scaling
    )
    value_grad = jnp.einsum(
        "sqgk,sqgd->skd", weight_four, grad_four, preferred_element_type=jnp.float32
    )
    return (query_grad.reshape(-1, own_keys.shape[2]), key_grad, value_grad)


def on_device(
    queries,
    cotangent,
    resp_keys,
    resp_values,
    prefix_keys,
    prefix_values,
    counts,
    lengths,
    policy_likelihood,
    reference_likelihood,
):
    group_size = HEADS // KV_HEADS
    group_width = group_size * HEAD_DIM
    scaling = 1.0 / math.sqrt(HEAD_DIM)
    slot_count = queries.shape[1]
    resp_len = queries.shape[2]
    local_keys = prefix_keys[0]
    local_values = prefix_values[0]
    prefix_len = local_keys.shape[0] * lax.axis_size("resp")
    live_count = counts[0]
    count_real = live_count.astype(jnp.float32)
    slot_ids = lax.axis_index("resp") * slot_count + jnp.arange(slot_count, dtype=jnp.int32)
    live_slots = slot_ids < live_count
    margin = policy_likelihood[0] - reference_likelihood[0]
    weight = jnp.where(live_slots, 2.0 * jax.nn.sigmoid(loss_beta * margin) / count_real, 0.0)
    loss_terms = jnp.where(live_slots, 2.0 / loss_beta * jax.nn.softplus(loss_beta * margin), 0.0)
    forget_loss = (lax.psum(jnp.sum(loss_terms), "resp") / count_real).reshape(1)
    positions = jnp.arange(resp_len, dtype=jnp.int32)
    kept_tokens = positions[None, :] < lengths[0][:, None]
    factor = jnp.where(kept_tokens, weight[:, None], 0.0)
    grad_out = (cotangent[0].astype(jnp.float32) * factor[:, :, None]).astype(jnp.bfloat16)
    query_fours, grad_fours, query_rows, grad_rows = ([], [], [], [])
    keys_own, scores_own, slopes_own = ([], [], [])
    for group_index in range(KV_HEADS):
        query_four = head_block(queries[0], group_index, group_width).reshape(
            slot_count, resp_len, group_size, HEAD_DIM
        )
        grad_four = head_block(grad_out, group_index, group_width).reshape(
            slot_count, resp_len, group_size, HEAD_DIM
        )
        own_keys = head_block(resp_keys[0], group_index, HEAD_DIM)
        own_values = head_block(resp_values[0], group_index, HEAD_DIM)
        query_fours.append(query_four)
        grad_fours.append(grad_four)
        query_rows.append(query_four.reshape(-1, HEAD_DIM))
        grad_rows.append(grad_four.reshape(-1, HEAD_DIM))
        keys_own.append(own_keys)
        scores_own.append(own_scores(query_four, own_keys, scaling))
        slopes_own.append(own_slopes(grad_four, own_values))
    query_grads, key_grads, value_grads = ([], [], [])
    start_peaks = jnp.stack(
        [jnp.max(scores_own[group_index], axis=1) for group_index in range(KV_HEADS)]
    )
    start_totals = jnp.stack(
        [
            jnp.sum(jnp.exp(scores_own[group_index] - start_peaks[group_index][:, None]), axis=1)
            for group_index in range(KV_HEADS)
        ]
    )
    arrived = lax.all_gather(local_keys, "resp", axis=0, tiled=True)
    peaks_out = []
    totals_out = []
    for add_group_index in range(KV_HEADS):
        scores_pre = (
            across_rows(query_rows[add_group_index], head_block(arrived, add_group_index, HEAD_DIM))
            * scaling
        )
        peaks_new = jnp.maximum(start_peaks[add_group_index], jnp.max(scores_pre, axis=1))
        totals_new = start_totals[add_group_index] * jnp.exp(
            start_peaks[add_group_index] - peaks_new
        ) + jnp.sum(jnp.exp(scores_pre - peaks_new[:, None]), axis=1)
        peaks_out.append(peaks_new)
        totals_out.append(totals_new)
    row_peaks = jnp.stack(peaks_out)
    totals = jnp.stack(totals_out)
    log_total = row_peaks + jnp.log(totals)
    weights_own = [
        jnp.exp(scores_own[group_index] - log_total[group_index][:, None])
        for group_index in range(KV_HEADS)
    ]
    start_centre = jnp.stack(
        [
            jnp.sum(weights_own[group_index] * slopes_own[group_index], axis=1)
            for group_index in range(KV_HEADS)
        ]
    )

    def add_centre(running, arrived):
        piece_keys, piece_values = arrived
        new_centre = []
        for group_index in range(KV_HEADS):
            scores_pre = (
                across_rows(query_rows[group_index], head_block(piece_keys, group_index, HEAD_DIM))
                * scaling
            )
            weights_pre = jnp.exp(scores_pre - log_total[group_index][:, None])
            slope_pre = across_rows(
                grad_rows[group_index], head_block(piece_values, group_index, HEAD_DIM)
            )
            new_centre.append(running[group_index] + jnp.sum(weights_pre * slope_pre, axis=1))
        return jnp.stack(new_centre)

    centre = add_centre(
        start_centre,
        (
            lax.all_gather(local_keys, "resp", axis=0, tiled=True),
            lax.all_gather(local_values, "resp", axis=0, tiled=True),
        ),
    )
    start_query = []
    for group_index in range(KV_HEADS):
        shift_mine = (
            weights_own[group_index] * (slopes_own[group_index] - centre[group_index][:, None])
        ).astype(jnp.bfloat16)
        query_grad, key_grad, value_grad = own_grads(
            shift_mine,
            weights_own[group_index],
            query_fours[group_index],
            grad_fours[group_index],
            keys_own[group_index],
            scaling,
        )
        start_query.append(query_grad)
        key_grads.append(key_grad)
        value_grads.append(value_grad)
    empty_rows = jnp.zeros((prefix_len, KV_HEADS * HEAD_DIM), jnp.float32)

    def add_terms(running, arrived):
        query_in, keys_in, values_in = running
        piece_keys, piece_values = arrived
        query_out, key_cols, value_cols = ([], [], [])
        for group_index in range(KV_HEADS):
            head_keys = head_block(piece_keys, group_index, HEAD_DIM)
            scores_pre = across_rows(query_rows[group_index], head_keys) * scaling
            weights_pre = jnp.exp(scores_pre - log_total[group_index][:, None])
            slope_pre = across_rows(
                grad_rows[group_index], head_block(piece_values, group_index, HEAD_DIM)
            )
            shift_pre = (weights_pre * (slope_pre - centre[group_index][:, None])).astype(
                jnp.bfloat16
            )
            query_out.append(
                query_in[group_index]
                + jnp.dot(shift_pre, head_keys, preferred_element_type=jnp.float32) * scaling
            )
            key_cols.append(down_columns(shift_pre, query_rows[group_index]) * scaling)
            value_cols.append(
                down_columns(weights_pre.astype(jnp.bfloat16), grad_rows[group_index])
            )
        keys_out = jnp.concatenate(key_cols, axis=1)
        values_out = jnp.concatenate(value_cols, axis=1)
        return (jnp.stack(query_out), keys_out, values_out)

    query_sum, partial_keys, partial_values = add_terms(
        (jnp.stack(start_query), empty_rows, empty_rows),
        (
            lax.all_gather(local_keys, "resp", axis=0, tiled=True),
            lax.all_gather(local_values, "resp", axis=0, tiled=True),
        ),
    )
    query_grads = [query_sum[group_index] for group_index in range(KV_HEADS)]
    grad_queries = jnp.concatenate(
        [
            query_grads[group_index].reshape(slot_count, resp_len, group_width)
            for group_index in range(KV_HEADS)
        ],
        axis=2,
    ).astype(jnp.bfloat16)
    grad_resp_keys = jnp.concatenate(key_grads, axis=2).astype(jnp.bfloat16)
    grad_resp_values = jnp.concatenate(value_grads, axis=2).astype(jnp.bfloat16)
    summed_keys, summed_values = (
        lax.psum_scatter(
            partial_keys.astype(jnp.bfloat16), "resp", scatter_dimension=0, tiled=True
        ).astype(jnp.float32),
        lax.psum_scatter(
            partial_values.astype(jnp.bfloat16), "resp", scatter_dimension=0, tiled=True
        ).astype(jnp.float32),
    )
    return (
        grad_queries[None],
        grad_resp_keys[None],
        grad_resp_values[None],
        summed_keys.astype(jnp.bfloat16)[None],
        summed_values.astype(jnp.bfloat16)[None],
        forget_loss,
    )


def solution(mesh):
    placed = (
        P(("groups", "prompt"), "resp", None, None),
        P(("groups", "prompt"), "resp", None, None),
        P(("groups", "prompt"), "resp", None, None),
        P(("groups", "prompt"), "resp", None, None),
        P(("groups", "prompt"), "resp", None),
        P(("groups", "prompt"), "resp", None),
        P(("groups", "prompt")),
        P(("groups", "prompt"), "resp"),
        P(("groups", "prompt"), "resp"),
        P(("groups", "prompt"), "resp"),
    )
    return jax.shard_map(
        on_device,
        mesh=mesh,
        in_specs=placed,
        out_specs=(
            P(("groups", "prompt"), "resp", None, None),
            P(("groups", "prompt"), "resp", None, None),
            P(("groups", "prompt"), "resp", None, None),
            P(("groups", "prompt"), "resp", None),
            P(("groups", "prompt"), "resp", None),
            P(("groups", "prompt")),
        ),
        check_vma=False,
    )
```

profile of v0, /device:TPU:0, one launch (start us, length us, event | category | flops | bytes accessed | tf_op | source)
XLA Modules:
  0.0 151.5 jit_solution(3817466985412128707)
XLA Ops:
  7.2 1.3 slice_bitcast_fusion.27
  17.3 17.4 %all-gather = bf16[1,512,512]{2,1,0:T(8,128)(2,1)S(1)} all-gather(bf16[1,128,512]{2,1,0:T(8,128)(2,1)S(1)} %copy-done.58), channel_id=2, replica_groups=mesh['groups'=2,'prompt'=4,'resp'=4] {'resp'}, dimensions={1}, use_global_device_ids=true | all-gather | bytes 655360 | tf_op jit(solution)/shard_map/all_gather | solution.py:128
  34.9 0.9 slice_bitcast_fusion.23
  45.7 1.2 fusion.74
  52.4 0.9 pad_maximum_fusion.2
  53.2 2.1 %copy.87 = bf16[512,512]{1,0:T(8,128)(2,1)} copy(bf16[512,512]{0,1:T(8,128)(2,1)} %pad_maximum_fusion.2) | data formatting | bytes 1048576
  55.4 19.7 %all-gather.1 = bf16[1,512,512]{2,1,0:T(8,128)(2,1)S(1)} all-gather(bf16[1,128,512]{2,1,0:T(8,128)(2,1)} %param.15), channel_id=3, replica_groups=mesh['groups'=2,'prompt'=4,'resp'=4] {'resp'}, dimensions={1}, use_global_device_ids=true | all-gather | bytes 655360 | tf_op jit(solution)/shard_map/all_gather | solution.py:175
  75.1 3.1 %multiply_reduce_fusion.3 = (f32[512]{0:T(512)}, f32[512,512]{0,1:T(8,128)}) fusion(f32[512,512]{0,1:T(8,128)} %copy-done, f32[512]{0:T(512)S(1)} %bitcast.309, bf16[512,128]{1,0:T(8,128)(2,1)S(1)} %dot_general.148, bf16[512,512]{1,0:T(8,128)(2,1)S(1)} %bitcast.255), kind=kOutput, calls=%fused_computation.80 | convolution fusion | flops 67894784 | bytes 2363392 | tf_op jit(solution)/shard_map/dot_general | solution.py:21
  78.3 1.9 %multiply_reduce_fusion.2 = (f32[512]{0:T(512)}, f32[512,512]{0,1:T(8,128)}) fusion(f32[512,512]{0,1:T(8,128)S(1)} %get-tuple-element.67, f32[512]{0:T(512)S(1)} %bitcast.304, bf16[512,128]{1,0:T(8,128)(2,1)S(1)} %copy-done.18, bf16[512,512]{1,0:T(8,128)(2,1)S(1)} %bitcast.256), kind=kOutput, calls=%fused_computation.77 | convolution fusion | flops 67894784 | bytes 2363392 | tf_op jit(solution)/shard_map/dot_general | solution.py:21
  80.2 1.9 %multiply_reduce_fusion.1 = (f32[512]{0:T(512)}, f32[512,512]{0,1:T(8,128)}) fusion(f32[512,512]{0,1:T(8,128)S(1)} %get-tuple-element.63, f32[512]{0:T(512)S(1)} %bitcast.299, bf16[512,128]{1,0:T(8,128)(2,1)S(1)} %copy-done.20, bf16[512,512]{1,0:T(8,128)(2,1)S(1)} %bitcast.257), kind=kOutput, calls=%fused_computation.74 | convolution fusion | flops 67894784 | bytes 2363392 | tf_op jit(solution)/shard_map/dot_general | solution.py:21
  82.0 1.9 %multiply_reduce_fusion = (f32[512]{0:T(512)}, f32[512,512]{0,1:T(8,128)}) fusion(f32[512,512]{0,1:T(8,128)S(1)} %get-tuple-element.59, f32[512]{0:T(512)S(1)} %bitcast.294, bf16[512,128]{1,0:T(8,128)(2,1)S(1)} %copy-done.22, bf16[512,512]{1,0:T(8,128)(2,1)S(1)} %bitcast.258), kind=kOutput, calls=%fused_computation.71 | convolution fusion | flops 67894784 | bytes 2363392 | tf_op jit(solution)/shard_map/dot_general | solution.py:21
  84.7 1.7 %copy.74 = f32[512,32]{0,1:T(8,128)} copy(f32[512,32]{1,0:T(8,128)} %bitcast.252) | data formatting | bytes 131072 | tf_op jit(solution)/shard_map/reshape | solution.py:40
  86.3 1.7 %copy.72 = f32[512,32]{0,1:T(8,128)} copy(f32[512,32]{1,0:T(8,128)} %bitcast.253) | data formatting | bytes 131072 | tf_op jit(solution)/shard_map/reshape | solution.py:40
  88.0 1.7 %copy.70 = f32[512,32]{0,1:T(8,128)} copy(f32[512,32]{1,0:T(8,128)} %bitcast.254) | data formatting | bytes 131072 | tf_op jit(solution)/shard_map/reshape | solution.py:40
  89.7 1.8 %multiply_reduce_fusion.4 = (f32[512]{0:T(512)S(1)}, f32[512,32]{0,1:T(8,128)}) fusion(f32[512,32]{0,1:T(8,128)} %copy.76, f32[512]{0:T(512)S(1)} %bitcast.295, bf16[512,128]{1,0:T(8,128)(2,1)} %dot_general.163, bf16[1,32,512]{2,1,0:T(8,128)(2,1)} %bitcast.313), kind=kOutput, calls=%fused_computation.126 | convolution fusion | flops 4242944 | bytes 274432 | tf_op jit(solution)/shard_map/sqgd,skd->sqgk/dot_general | solution.py:45
  91.5 1.7 %multiply_reduce_fusion.5 = (f32[512]{0:T(512)S(1)}, f32[512,32]{0,1:T(8,128)}) fusion(f32[512,32]{0,1:T(8,128)} %copy.74, f32[512]{0:T(512)S(1)} %bitcast.300, bf16[512,128]{1,0:T(8,128)(2,1)} %dot_general.158, bf16[1,32,512]{2,1,0:T(8,128)(2,1)} %bitcast.314), kind=kOutput, calls=%fused_computation.129 | convolution fusion | flops 4242944 | bytes 274432 | tf_op jit(solution)/shard_map/sqgd,skd->sqgk/dot_general | solution.py:45
  93.2 1.7 %multiply_reduce_fusion.6 = (f32[512]{0:T(512)S(1)}, f32[512,32]{0,1:T(8,128)}) fusion(f32[512,32]{0,1:T(8,128)} %copy.72, f32[512]{0:T(512)S(1)} %bitcast.305, bf16[512,128]{1,0:T(8,128)(2,1)} %dot_general.153, bf16[1,32,512]{2,1,0:T(8,128)(2,1)} %bitcast.315), kind=kOutput, calls=%fused_computation.132 | convolution fusion | flops 4242944 | bytes 274432 | tf_op jit(solution)/shard_map/sqgd,skd->sqgk/dot_general | solution.py:45
  94.9 1.6 %multiply_reduce_fusion.7 = (f32[512]{0:T(512)S(1)}, f32[512,32]{0,1:T(8,128)}) fusion(f32[512,32]{0,1:T(8,128)} %copy.70, f32[512]{0:T(512)S(1)} %bitcast.310, bf16[512,128]{1,0:T(8,128)(2,1)S(1)} %dot_general.148, bf16[1,32,512]{2,1,0:T(8,128)(2,1)} %bitcast.316), kind=kOutput, calls=%fused_computation.135 | convolution fusion | flops 4242944 | bytes 274432 | tf_op jit(solution)/shard_map/sqgd,skd->sqgk/dot_general | solution.py:45
  97.2 1.6 %multiply_convert_fusion.3 = bf16[512,512]{0,1:T(8,128)(2,1)S(1)} fusion(f32[512,512]{0,1:T(8,128)} %get-tuple-element.87, f32[512,512]{0,1:T(8,128)S(1)} %copy-done.1, f32[512]{0:T(512)S(1)} %add.106, f32[512]{0:T(512)S(1)} %bitcast.311), kind=kLoop, calls=%fused_computation.79 | loop fusion | flops 1048576 | bytes 2625536 | tf_op jit(solution)/shard_map/convert_element_type | solution.py:207
  103.8 0.9 pad_maximum_fusion.1
  104.7 0.8 copy-done.36
  106.5 0.8 fusion.35
  109.1 0.8 fusion.34
  111.6 0.8 fusion.33
  112.4 0.9 convolution_multiply_fusion.11
  114.2 0.8 fusion.32
  115.0 0.9 convolution_multiply_fusion.9
  120.1 1.0 fusion.15
  127.3 12.0 %psum.7 = f32[]{:T(128)} all-reduce(f32[]{:T(128)} %bitcast.64), channel_id=1, replica_groups=mesh['groups'=2,'prompt'=4,'resp'=4] {'resp'}, use_global_device_ids=true, to_apply=%region_26.27 | all-reduce | flops 1 | bytes 8 | tf_op jit(solution)/shard_map/psum | solution.py:95
  140.9 0.8 pad_maximum_fusion
  141.7 1.0 copy.88
  142.8 0.8 copy.82
  (270 shorter events, 44.2 us)
Async XLA Ops:
  7.2 134.6 %reduce-scatter.7.cloned.1.call-start = ((), (), s32[]{:S(2)}) async-start(), calls=%async_computation.3 | async-start | bytes 655360
  10.4 30.2 %copy-start.11 = (f32[32,16,32]{2,1,0:T(8,128)}, f32[32,16,32]{2,1,0:T(8,128)S(1)}, u32[]{:S(2)}) copy-start(f32[32,16,32]{2,1,0:T(8,128)S(1)} %get-tuple-element.61) | copy-start | bytes 196612
  11.8 29.7 %copy-start.13 = (f32[32,16,32]{2,1,0:T(8,128)}, f32[32,16,32]{2,1,0:T(8,128)S(1)}, u32[]{:S(2)}) copy-start(f32[32,16,32]{2,1,0:T(8,128)S(1)} %get-tuple-element.65) | copy-start | bytes 196612
  12.6 4.7 %copy-start.58 = (bf16[1,128,512]{2,1,0:T(8,128)(2,1)S(1)}, bf16[1,128,512]{2,1,0:T(8,128)(2,1)}, u32[]{:S(2)}) copy-start(bf16[1,128,512]{2,1,0:T(8,128)(2,1)} %param.14) | copy-start | bytes 393220
  12.7 22.1 %copy-start.52 = (bf16[1,1,32,8192]{3,2,1,0:T(8,128)(2,1)S(1)}, bf16[1,1,32,8192]{3,2,1,0:T(8,128)(2,1)}, u32[]{:S(2)}) copy-start(bf16[1,1,32,8192]{3,2,1,0:T(8,128)(2,1)} %param.11) | copy-start | bytes 1572868
  13.3 29.2 %copy-start.15 = (f32[32,16,32]{2,1,0:T(8,128)}, f32[32,16,32]{2,1,0:T(8,128)S(1)}, u32[]{:S(2)}) copy-start(f32[32,16,32]{2,1,0:T(8,128)S(1)} %get-tuple-element.69) | copy-start | bytes 196612
  34.7 9.4 %copy-start.6 = (bf16[1,512,512]{2,1,0:T(8,128)(2,1)}, bf16[1,512,512]{2,1,0:T(8,128)(2,1)S(1)}, u32[]{:S(2)}) copy-start(bf16[1,512,512]{2,1,0:T(8,128)(2,1)S(1)} %all-gather) | copy-start | bytes 1572868
  39.6 4.1 %copy-start.27 = (bf16[512,128]{1,0:T(8,128)(2,1)}, bf16[512,128]{1,0:T(8,128)(2,1)S(1)}, u32[]{:S(2)}) copy-start(bf16[512,128]{1,0:T(8,128)(2,1)S(1)} %reshape_reshape.17) | copy-start | bytes 393220
  39.7 3.7 %copy-start.29 = (bf16[512,128]{1,0:T(8,128)(2,1)}, bf16[512,128]{1,0:T(8,128)(2,1)S(1)}, u32[]{:S(2)}) copy-start(bf16[512,128]{1,0:T(8,128)(2,1)S(1)} %reshape_reshape.16) | copy-start | bytes 393220
  43.7 8.3 %copy-start = (f32[512,512]{0,1:T(8,128)}, f32[512,512]{0,1:T(8,128)S(1)}, u32[]{:S(2)}) copy-start(f32[512,512]{0,1:T(8,128)S(1)} %get-tuple-element.71) | copy-start | bytes 3145732
  55.4 88.2 %reduce-scatter.5.cloned.1.call-start = ((), (), s32[]{:S(2)}) async-start(), calls=%async_computation.2 | async-start | bytes 655360 | tf_op jit(solution)/shard_map/reduce_scatter | solution.py:240
  75.1 3.1 %copy-start.18 = (bf16[512,128]{1,0:T(8,128)(2,1)S(1)}, bf16[512,128]{1,0:T(8,128)(2,1)}, u32[]{:S(2)}) copy-start(bf16[512,128]{1,0:T(8,128)(2,1)} %dot_general.153) | copy-start | bytes 393220
  78.3 1.9 %copy-start.20 = (bf16[512,128]{1,0:T(8,128)(2,1)S(1)}, bf16[512,128]{1,0:T(8,128)(2,1)}, u32[]{:S(2)}) copy-start(bf16[512,128]{1,0:T(8,128)(2,1)} %dot_general.158) | copy-start | bytes 393220
  80.2 1.9 %copy-start.22 = (bf16[512,128]{1,0:T(8,128)(2,1)S(1)}, bf16[512,128]{1,0:T(8,128)(2,1)}, u32[]{:S(2)}) copy-start(bf16[512,128]{1,0:T(8,128)(2,1)} %dot_general.163) | copy-start | bytes 393220
  89.7 7.5 %copy-start.1 = (f32[512,512]{0,1:T(8,128)S(1)}, f32[512,512]{0,1:T(8,128)}, u32[]{:S(2)}) copy-start(f32[512,512]{0,1:T(8,128)} %copy-done) | copy-start | bytes 3145732
  97.2 1.6 %copy-start.30 = (bf16[512,128]{1,0:T(8,128)(2,1)S(1)}, bf16[512,128]{1,0:T(8,128)(2,1)}, u32[]{:S(2)}) copy-start(bf16[512,128]{1,0:T(8,128)(2,1)} %copy-done.29) | copy-start | bytes 393220
  97.2 2.6 %copy-start.10 = (f32[512,512]{0,1:T(8,128)S(1)}, f32[512,512]{0,1:T(8,128)}, u32[]{:S(2)}) copy-start(f32[512,512]{0,1:T(8,128)} %get-tuple-element.83) | copy-start | bytes 3145732
  98.8 1.3 copy-start.2
  99.8 1.3 copy-start.9
  100.1 1.7 %copy-start.4 = (bf16[512,512]{0,1:T(8,128)(2,1)}, bf16[512,512]{0,1:T(8,128)(2,1)S(1)}, u32[]{:S(2)}) copy-start(bf16[512,512]{0,1:T(8,128)(2,1)S(1)} %multiply_convert_fusion.2) | copy-start | bytes 1572868
  101.4 1.3 copy-start.8
  114.2 1.7 %copy-start.48 = (bf16[4,8,16,128]{3,1,2,0:T(8,128)(2,1)S(1)}, bf16[4,8,16,128]{3,1,2,0:T(8,128)(2,1)}, u32[]{:S(2)}) copy-start(bf16[4,8,16,128]{3,1,2,0:T(8,128)(2,1)} %get-tuple-element.36) | copy-start | bytes 393220
  115.0 1.6 %copy-start.47 = (bf16[4,8,16,128]{3,1,2,0:T(8,128)(2,1)S(1)}, bf16[4,8,16,128]{3,1,2,0:T(8,128)(2,1)}, u32[]{:S(2)}) copy-start(bf16[4,8,16,128]{3,1,2,0:T(8,128)(2,1)} %get-tuple-element.37) | copy-start | bytes 393220
  115.0 2.2 %copy-start.46 = (bf16[4,8,16,128]{3,1,2,0:T(8,128)(2,1)S(1)}, bf16[4,8,16,128]{3,1,2,0:T(8,128)(2,1)}, u32[]{:S(2)}) copy-start(bf16[4,8,16,128]{3,1,2,0:T(8,128)(2,1)} %get-tuple-element.38) | copy-start | bytes 393220
  115.0 2.9 %copy-start.45 = (bf16[4,8,16,128]{3,1,2,0:T(8,128)(2,1)S(1)}, bf16[4,8,16,128]{3,1,2,0:T(8,128)(2,1)}, u32[]{:S(2)}) copy-start(bf16[4,8,16,128]{3,1,2,0:T(8,128)(2,1)} %get-tuple-element.39) | copy-start | bytes 393220
  115.9 2.1 %copy-start.71 = (f32[512]{0:T(512)S(1)}, f32[512]{0:T(512)}, u32[]{:S(2)}) copy-start(f32[512]{0:T(512)} %get-tuple-element.24) | copy-start | bytes 6148
  115.9 4.2 %copy-start.3 = (bf16[512,512]{0,1:T(8,128)(2,1)S(1)}, bf16[512,512]{0,1:T(8,128)(2,1)}, u32[]{:S(2)}) copy-start(bf16[512,512]{0,1:T(8,128)(2,1)} %copy-done.2) | copy-start | bytes 1572868
  115.9 4.2 %copy-start.7 = (bf16[1,512,512]{2,1,0:T(8,128)(2,1)S(1)}, bf16[1,512,512]{2,1,0:T(8,128)(2,1)}, u32[]{:S(2)}) copy-start(bf16[1,512,512]{2,1,0:T(8,128)(2,1)} %copy-done.6) | copy-start | bytes 1572868
  117.2 1.4 copy-start.70
  117.2 2.1 %copy-start.69 = (f32[512]{0:T(512)S(1)}, f32[512]{0:T(512)}, u32[]{:S(2)}) copy-start(f32[512]{0:T(512)} %get-tuple-element.26) | copy-start | bytes 6148
  117.2 2.8 %copy-start.68 = (f32[512]{0:T(512)S(1)}, f32[512]{0:T(512)}, u32[]{:S(2)}) copy-start(f32[512]{0:T(512)} %get-tuple-element.27) | copy-start | bytes 6148
  126.2 13.0 %copy-start.53 = (bf16[512,128]{1,0:T(8,128)(2,1)S(1)}, bf16[512,128]{1,0:T(8,128)(2,1)}, u32[]{:S(2)}) copy-start(bf16[512,128]{1,0:T(8,128)(2,1)} %fusion.15) | copy-start | bytes 393220
  (54 other events, 46.4 us)
Sparse Core Ops, SparseCore 0:
  55.5 24.7 reduce-scatter.6
  104.9 21.6 reduce-scatter.4
where the time goes:
time: 153 us; the launch traced here: 152 us
  blocking collectives  49.1 us (32%)
  local copies, waits for them, and re-layouts  44.7 us (29%)
  matrix products  29.8 us (19%)
  between operations  19.5 us (13%)
  other arithmetic  8.31 us (5%)
    unnamed x181, local copies, waits for them, and re-layouts  25.9 us
    all_gather x1, blocking collectives, on_device(): lax.all_gather(local_values, 'resp', axis=0, tiled=True)  19.7 us
    all_gather x1, blocking collectives, on_device(): arrived = lax.all_gather(local_keys, 'resp', axis=0, tiled=True)  17.4 us
    psum x1, blocking collectives, on_device(): lax.psum(jnp.sum(loss_terms), 'resp') / count_real  12 us
    dot_general x8, matrix products, across_rows(): lax.dot_general(left_side, right_side, (((1,), (1,)), ((), ())), preferre...  10.9 us
    dot_general x4, matrix products, own_slopes(): jnp.einsum('sqgd,skd->sqgk', grad_four, own_values, preferred_element_typ...  6.84 us
    reshape x4, local copies, waits for them, and re-layouts, own_scores(): jnp.where(causal[None, :, None, :], scores, masked_score)  5.78 us
    dot_general x4, matrix products, own_grads(): jnp.einsum('sqgk,sqgd->skd', shift_four, query_four, preferred_element_ty...  3.16 us
  transfers between devices with their start and end apart: 2, of which 0 were waited for; matrix products, arithmetic and copies ran while one was open for 29% of the time, Pallas kernels for 0%

commit v1 on v0

--- a/solution.py
+++ b/solution.py
@@ -9,6 +9,27 @@
 HEAD_DIM = 128
 loss_beta = 0.5
 masked_score = -1e30
+
+
+def ring_gather(x, axis, dim):
+    size, here, rows = (lax.axis_size(axis), lax.axis_index(axis), x.shape[dim])
+    upward = [(i, (i + 1) % size) for i in range(size)]
+    behind = [(i, (i - 1) % size) for i in range(size)]
+    filled = jnp.zeros((*x.shape[:dim], size * rows, *x.shape[dim + 1 :]), x.dtype)
+    filled = lax.dynamic_update_slice_in_dim(filled, x, here * rows, axis=dim)
+    from_left = from_right = x
+    middle = size // 2
+    for turn in range(1, middle + 1):
+        from_left = lax.ppermute(from_left, axis, upward)
+        filled = lax.dynamic_update_slice_in_dim(
+            filled, from_left, (here - turn) % size * rows, axis=dim
+        )
+        if turn < size - middle:
+            from_right = lax.ppermute(from_right, axis, behind)
+            filled = lax.dynamic_update_slice_in_dim(
+                filled, from_right, (here + turn) % size * rows, axis=dim
+            )
+    return filled
 
 
 def head_block(values_in, position, column_span):
@@ -172,7 +193,7 @@
         start_centre,
         (
             lax.all_gather(local_keys, "resp", axis=0, tiled=True),
-            lax.all_gather(local_values, "resp", axis=0, tiled=True),
+            ring_gather(local_values, "resp", 0),
         ),
     )
     start_query = []

time: 153 us -> 192 us (1.25)
  waiting for transfers between devices: 0.04 us -> 17.4 us
  local copies, waits for them, and re-layouts: 44.7 us -> 58.8 us
  starting transfers between devices: 0.08 us -> 6.11 us
  matrix products: 29.8 us -> 35 us
  blocking collectives: 49.1 us -> 45.9 us
    reduce_scatter x1, waiting for transfers between devices: 0.01 us -> 14.1 us  [on_device(): lax.psum_scatter(partial_keys.astype(jnp.bfloat16), 'resp', scatter_dimen...]
    ppermute x0 -> x3, starting transfers between devices: none -> 6.03 us  [the longest x2 3.94 us: ring_gather(): from_left = lax.ppermute(from_left, axis, upward)]
    convert_element_type x4, local copies, waits for them, and re-layouts: 0.48 us -> 4.67 us  [on_device(): shift_mine = (weights_own[group_index] * (slopes_own[group_index] - centr...]
    dot_general x4, matrix products: 2.03 us -> 5.95 us  [own_grads(): jnp.einsum('sqgk,skd->sqgd', shift_four, own_keys, preferred_element_type...]
    dynamic_update_slice x0 -> x4, local copies, waits for them, and re-layouts: none -> 3.84 us  [the longest x2 2.25 us: ring_gather(): lax.dynamic_update_slice_in_dim(filled, from_left, (here - turn) % size *...]
    unnamed x181 -> x203, local copies, waits for them, and re-layouts: 25.9 us -> 29.5 us
    sub x4, local copies, waits for them, and re-layouts: 2.13 us -> 5.43 us  [on_device(): scores_own[group_index] - log_total[group_index][:, None]]
    ppermute x0 -> x3, waiting for transfers between devices: none -> 3.18 us  [the longest x2 3.18 us: ring_gather(): from_left = lax.ppermute(from_left, axis, upward)]
  transfers between devices with their start and end apart: 2 -> 5, of which waited for: 0 -> 2; matrix products, arithmetic and copies ran while one was open for 29% -> 43% of each run, Pallas kernels for 0% -> 0%
where the time goes in v1:
time: 192 us; the launch traced here: 190 us
  local copies, waits for them, and re-layouts  58.8 us (31%)
  blocking collectives  45.9 us (24%)
  matrix products  35 us (18%)
  between operations  19.5 us (10%)
  waiting for transfers between devices  17.4 us (9%)
  other arithmetic  7.73 us (4%)
  starting transfers between devices  6.11 us (3%)
    unnamed x203, local copies, waits for them, and re-layouts  29.5 us
    all_gather x1, blocking collectives, on_device(): lax.all_gather(local_values, 'resp', axis=0, tiled=True)  19.5 us
    all_gather x1, blocking collectives, on_device(): arrived = lax.all_gather(local_keys, 'resp', axis=0, tiled=True)  15.6 us
    reduce_scatter x1, waiting for transfers between devices, on_device(): lax.psum_scatter(partial_keys.astype(jnp.bfloat16), 'resp', scatter_dimen...  14.1 us
    psum x1, blocking collectives, on_device(): lax.psum(jnp.sum(loss_terms), 'resp') / count_real  10.8 us
    dot_general x12, matrix products, across_rows(): lax.dot_general(left_side, right_side, (((1,), (1,)), ((), ())), preferre...  10.3 us
    dot_general x4, matrix products, own_slopes(): jnp.einsum('sqgd,skd->sqgk', grad_four, own_values, preferred_element_typ...  6.36 us
    dot_general x4, matrix products, own_grads(): jnp.einsum('sqgk,skd->sqgd', shift_four, own_keys, preferred_element_type...  5.95 us
  transfers between devices with their start and end apart: 5, of which 2 were waited for; matrix products, arithmetic and copies ran while one was open for 43% of the time, Pallas kernels for 0%

profile of v1, /device:TPU:0, one launch (start us, length us, event | category | flops | bytes accessed | tf_op | source)
XLA Modules:
  0.0 190.4 jit_solution(6580974347387769982)
XLA Ops:
  7.2 3.1 %collective-permute-start = (bf16[128,512]{1,0:T(8,128)(2,1)}, bf16[128,512]{1,0:T(8,128)(2,1)}, u32[]{:S(2)}, u32[]{:S(2)}) collective-permute-start(bf16[128,512]{1,0:T(8,128)(2,1)} %bitcast.278), channel_id=1, source_target_pairs={{0,1},{1,2},{2,3},{3,0},{4,5},{5,6},{6,7},{7,4},{8,9},{9,10},{10,1... | collective-permute-start | bytes 393224 | tf_op jit(solution)/shard_map/ppermute | solution.py:23
  10.3 2.1 %collective-permute-start.1 = (bf16[128,512]{1,0:T(8,128)(2,1)}, bf16[128,512]{1,0:T(8,128)(2,1)}, u32[]{:S(2)}, u32[]{:S(2)}) collective-permute-start(bf16[128,512]{1,0:T(8,128)(2,1)} %bitcast.279), channel_id=1, source_target_pairs={{0,3},{1,0},{2,1},{3,2},{4,7},{5,4},{6,5},{7,6},{8,11},{9,8},{10,9... | collective-permute-start | bytes 393224 | tf_op jit(solution)/shard_map/ppermute | solution.py:28
  22.5 15.6 %all-gather = bf16[1,512,512]{2,1,0:T(8,128)(2,1)S(1)} all-gather(bf16[1,128,512]{2,1,0:T(8,128)(2,1)S(1)} %copy-done.64), channel_id=2, replica_groups=mesh['groups'=2,'prompt'=4,'resp'=4] {'resp'}, dimensions={1}, use_global_device_ids=true | all-gather | bytes 655360 | tf_op jit(solution)/shard_map/all_gather | solution.py:149
  56.6 2.0 %copy.103 = bf16[512,512]{1,0:T(8,128)(2,1)} copy(bf16[512,512]{0,1:T(8,128)(2,1)} %pad_maximum_fusion.2) | data formatting | bytes 1048576
  58.7 19.5 %all-gather.1 = bf16[1,512,512]{2,1,0:T(8,128)(2,1)} all-gather(bf16[1,128,512]{2,1,0:T(8,128)(2,1)} %param.15), channel_id=3, replica_groups=mesh['groups'=2,'prompt'=4,'resp'=4] {'resp'}, dimensions={1}, use_global_device_ids=true | all-gather | bytes 655360 | tf_op jit(solution)/shard_map/all_gather | solution.py:247
  78.2 1.6 copy.109
  83.2 1.7 copy.84
  84.8 1.7 copy.81
  86.5 1.7 copy.78
  88.2 1.4 sub.365
  89.6 1.4 sub.368
  92.3 1.4 sub.374
  93.7 2.3 %multiply_reduce_fusion = (f32[512]{0:T(512)}, f32[512,32]{0,1:T(8,128)}) fusion(f32[512,32]{0,1:T(8,128)} %copy.87, f32[512]{0:T(512)S(1)} %bitcast.302, bf16[512,128]{1,0:T(8,128)(2,1)S(1)} %dot_general.174, bf16[1,32,512]{2,1,0:T(8,128)(2,1)} %bitcast.321), kind=kOutput, calls=%fused_computation.138 | convolution fusion | flops 4242944 | bytes 274432 | tf_op jit(solution)/shard_map/sqgd,skd->sqgk/dot_general | solution.py:66
  95.9 1.4 multiply_reduce_fusion.1
  97.3 1.4 multiply_reduce_fusion.2
  98.7 1.4 multiply_reduce_fusion.3
  105.8 10.8 %psum.7 = f32[]{:T(128)} all-reduce(f32[]{:T(128)} %bitcast.65), channel_id=1, replica_groups=mesh['groups'=2,'prompt'=4,'resp'=4] {'resp'}, use_global_device_ids=true, to_apply=%region_26.27 | all-reduce | flops 1 | bytes 8 | tf_op jit(solution)/shard_map/psum | solution.py:116
  118.2 1.6 constant_dynamic-update-slice_fusion.2
  119.8 1.6 constant_dynamic-update-slice_fusion.1
  121.4 3.2 %collective-permute-done.2 = bf16[128,512]{1,0:T(8,128)(2,1)S(1)} collective-permute-done((bf16[128,512]{1,0:T(8,128)(2,1)}, bf16[128,512]{1,0:T(8,128)(2,1)S(1)}, u32[]{:S(2)}, u32[]{:S(2)}) %collective-permute-start.2) | collective-permute-done | bytes 131104 | tf_op jit(solution)/shard_map/ppermute | solution.py:23
  125.2 1.9 fusion.11
  131.0 1.5 copy.85
  132.6 1.8 fusion.45
  134.4 1.6 convolution_multiply_fusion.15
  137.2 1.5 copy.82
  138.7 1.8 fusion.46
  140.5 1.6 convolution_multiply_fusion.17
  143.4 1.5 copy.79
  144.9 1.8 fusion.47
  146.7 1.8 convolution_multiply_fusion.19
  148.6 2.3 %fusion.5 = bf16[512,512]{0,1:T(8,128)(2,1)} fusion(bf16[512,128]{1,0:T(8,128)(2,1)S(1)} %copy-done.21, f32[512,512]{0,1:T(8,128)} %copy-done, f32[512]{0:T(512)S(1)} %copy-done.72, f32[512]{0:T(512)S(1)} %bitcast.320, bf16[512,512]{1,0:T(8,128)(2,1)S(1)} %bitcast.261), kind=kOutput, calls=%fused_computation.17 | convolution fusion | flops 68157440 | bytes 1839104 | tf_op jit(solution)/shard_map/dot_general | solution.py:42
  168.3 14.1 %reduce-scatter.5.cloned.1.call-done = bf16[128,512]{1,0:T(8,128)(2,1)} async-done(((bf16[512,512]{1,0:T(8,128)(2,1)}), bf16[128,512]{1,0:T(8,128)(2,1)}) %reduce-scatter.5.cloned.1.call-update) | async-done | bytes 131088 | tf_op jit(solution)/shard_map/reduce_scatter | solution.py:261
  (303 shorter events, 61.1 us)
Async XLA Ops:
  7.2 159.4 %reduce-scatter.7.cloned.1.call-start = ((), (), s32[]{:S(2)}) async-start(), calls=%async_computation.3 | async-start | bytes 655360
  7.2 110.1 %collective-permute-start = (bf16[128,512]{1,0:T(8,128)(2,1)}, bf16[128,512]{1,0:T(8,128)(2,1)}, u32[]{:S(2)}, u32[]{:S(2)}) collective-permute-start(bf16[128,512]{1,0:T(8,128)(2,1)} %bitcast.278), channel_id=1, source_target_pairs={{0,1},{1,2},{2,3},{3,0},{4,5},{5,6},{6,7},{7,4},{8,9},{9,10},{10,1... | collective-permute-start | bytes 393224 | tf_op jit(solution)/shard_map/ppermute | solution.py:23
  10.3 109.5 %collective-permute-start.1 = (bf16[128,512]{1,0:T(8,128)(2,1)}, bf16[128,512]{1,0:T(8,128)(2,1)}, u32[]{:S(2)}, u32[]{:S(2)}) collective-permute-start(bf16[128,512]{1,0:T(8,128)(2,1)} %bitcast.279), channel_id=1, source_target_pairs={{0,3},{1,0},{2,1},{3,2},{4,7},{5,4},{6,5},{7,6},{8,11},{9,8},{10,9... | collective-permute-start | bytes 393224 | tf_op jit(solution)/shard_map/ppermute | solution.py:28
  15.6 27.7 %copy-start.6 = (f32[32,16,32]{2,1,0:T(8,128)}, f32[32,16,32]{2,1,0:T(8,128)S(1)}, u32[]{:S(2)}) copy-start(f32[32,16,32]{2,1,0:T(8,128)S(1)} %get-tuple-element.61) | copy-start | bytes 196612
  17.0 27.2 %copy-start.8 = (f32[32,16,32]{2,1,0:T(8,128)}, f32[32,16,32]{2,1,0:T(8,128)S(1)}, u32[]{:S(2)}) copy-start(f32[32,16,32]{2,1,0:T(8,128)S(1)} %get-tuple-element.65) | copy-start | bytes 196612
  17.8 4.7 %copy-start.64 = (bf16[1,128,512]{2,1,0:T(8,128)(2,1)S(1)}, bf16[1,128,512]{2,1,0:T(8,128)(2,1)}, u32[]{:S(2)}) copy-start(bf16[1,128,512]{2,1,0:T(8,128)(2,1)} %param.14) | copy-start | bytes 393220
  17.8 20.3 %copy-start.58 = (bf16[1,1,32,8192]{3,2,1,0:T(8,128)(2,1)S(1)}, bf16[1,1,32,8192]{3,2,1,0:T(8,128)(2,1)}, u32[]{:S(2)}) copy-start(bf16[1,1,32,8192]{3,2,1,0:T(8,128)(2,1)} %param.11) | copy-start | bytes 1572868
  18.4 26.6 %copy-start.10 = (f32[32,16,32]{2,1,0:T(8,128)}, f32[32,16,32]{2,1,0:T(8,128)S(1)}, u32[]{:S(2)}) copy-start(f32[32,16,32]{2,1,0:T(8,128)S(1)} %get-tuple-element.69) | copy-start | bytes 196612
  38.1 8.6 %copy-start.4 = (bf16[1,512,512]{2,1,0:T(8,128)(2,1)}, bf16[1,512,512]{2,1,0:T(8,128)(2,1)S(1)}, u32[]{:S(2)}) copy-start(bf16[1,512,512]{2,1,0:T(8,128)(2,1)S(1)} %all-gather) | copy-start | bytes 1572868
  42.2 4.4 %copy-start.27 = (bf16[512,128]{1,0:T(8,128)(2,1)}, bf16[512,128]{1,0:T(8,128)(2,1)S(1)}, u32[]{:S(2)}) copy-start(bf16[512,128]{1,0:T(8,128)(2,1)S(1)} %reshape_reshape.18) | copy-start | bytes 393220
  42.3 4.0 %copy-start.29 = (bf16[512,128]{1,0:T(8,128)(2,1)}, bf16[512,128]{1,0:T(8,128)(2,1)S(1)}, u32[]{:S(2)}) copy-start(bf16[512,128]{1,0:T(8,128)(2,1)S(1)} %reshape_reshape.17) | copy-start | bytes 393220
  42.3 3.6 %copy-start.31 = (bf16[512,128]{1,0:T(8,128)(2,1)}, bf16[512,128]{1,0:T(8,128)(2,1)S(1)}, u32[]{:S(2)}) copy-start(bf16[512,128]{1,0:T(8,128)(2,1)S(1)} %reshape_reshape.16) | copy-start | bytes 393220
  47.5 5.5 %copy-start = (f32[512,512]{0,1:T(8,128)}, f32[512,512]{0,1:T(8,128)S(1)}, u32[]{:S(2)}) copy-start(f32[512,512]{0,1:T(8,128)S(1)} %get-tuple-element.63) | copy-start | bytes 3145732
  58.7 123.8 %reduce-scatter.5.cloned.1.call-start = ((), (), s32[]{:S(2)}) async-start(), calls=%async_computation.2 | async-start | bytes 655360 | tf_op jit(solution)/shard_map/reduce_scatter | solution.py:261
  93.6 2.3 %copy-start.19 = (bf16[512,128]{1,0:T(8,128)(2,1)S(1)}, bf16[512,128]{1,0:T(8,128)(2,1)}, u32[]{:S(2)}) copy-start(bf16[512,128]{1,0:T(8,128)(2,1)} %dot_general.168) | copy-start | bytes 393220
  93.6 2.3 %copy-start.41 = (f32[512,32]{0,1:T(8,128)S(1)}, f32[512,32]{0,1:T(8,128)}, u32[]{:S(2)}) copy-start(f32[512,32]{0,1:T(8,128)} %copy.84) | copy-start | bytes 196612
  93.7 2.3 %copy-start.70 = (bf16[1,1,32,512]{3,2,1,0:T(8,128)(2,1)S(1)}, bf16[1,1,32,512]{3,2,1,0:T(8,128)(2,1)}, u32[]{:S(2)}) copy-start(bf16[1,1,32,512]{3,2,1,0:T(8,128)(2,1)} %param.13) | copy-start | bytes 98308
  101.0 3.2 %copy-start.23 = (bf16[512,512]{1,0:T(8,128)(2,1)}, bf16[512,512]{1,0:T(8,128)(2,1)S(1)}, u32[]{:S(2)}) copy-start(bf16[512,512]{1,0:T(8,128)(2,1)S(1)} %constant_dynamic-update-slice_fusion.3) | copy-start | bytes 1572868
  117.3 9.8 %copy-start.1 = (f32[512,512]{0,1:T(8,128)S(1)}, f32[512,512]{0,1:T(8,128)}, u32[]{:S(2)}) copy-start(f32[512,512]{0,1:T(8,128)} %copy-done) | copy-start | bytes 3145732
  117.3 7.2 %collective-permute-start.2 = (bf16[128,512]{1,0:T(8,128)(2,1)}, bf16[128,512]{1,0:T(8,128)(2,1)S(1)}, u32[]{:S(2)}, u32[]{:S(2)}) collective-permute-start(bf16[128,512]{1,0:T(8,128)(2,1)} %collective-permute-done), channel_id=1, source_target_pairs={{0,1},{1,2},{2,3},{3,0},{4,5},{5,6},{6,7},{7,4},{8,9},{9,10},{10,1... | collective-permute-start | bytes 393224 | tf_op jit(solution)/shard_map/ppermute | solution.py:23
  125.2 1.9 copy-start.20
  125.2 1.9 copy-start.24
  132.6 1.8 copy-start.43
  134.4 2.2 %copy-start.40 = (f32[512,32]{0,1:T(8,128)S(1)}, f32[512,32]{0,1:T(8,128)}, u32[]{:S(2)}) copy-start(f32[512,32]{0,1:T(8,128)} %copy.81) | copy-start | bytes 196612
  134.4 2.2 %copy-start.62 = (f32[512,32]{0,1:T(8,128)S(1)}, f32[512,32]{0,1:T(8,128)}, u32[]{:S(2)}) copy-start(f32[512,32]{0,1:T(8,128)} %get-tuple-element.77) | copy-start | bytes 196612
  138.7 1.8 copy-start.44
  140.5 2.2 %copy-start.38 = (f32[512,32]{0,1:T(8,128)S(1)}, f32[512,32]{0,1:T(8,128)}, u32[]{:S(2)}) copy-start(f32[512,32]{0,1:T(8,128)} %copy.78) | copy-start | bytes 196612
  140.5 2.2 %copy-start.61 = (f32[512,32]{0,1:T(8,128)S(1)}, f32[512,32]{0,1:T(8,128)}, u32[]{:S(2)}) copy-start(f32[512,32]{0,1:T(8,128)} %get-tuple-element.79) | copy-start | bytes 196612
  144.9 3.7 %copy-start.22 = (bf16[1,512,512]{2,1,0:T(8,128)(2,1)S(1)}, bf16[1,512,512]{2,1,0:T(8,128)(2,1)}, u32[]{:S(2)}) copy-start(bf16[1,512,512]{2,1,0:T(8,128)(2,1)} %all-gather.1) | copy-start | bytes 1572868
  146.7 1.8 copy-start.21
  146.7 1.8 copy-start.72
  148.6 2.3 %copy-start.74 = (f32[512]{0:T(512)S(1)}, f32[512]{0:T(512)}, u32[]{:S(2)}) copy-start(f32[512]{0:T(512)} %copy-done.73) | copy-start | bytes 6148
  (68 other events, 66.6 us)
Sparse Core Ops, SparseCore 0:
  58.8 22.9 reduce-scatter.6
  162.5 19.9 reduce-scatter.4
